TPU v7x, 512 devices: a whole 4x8x8 slice. The times are simulated.
512 devices in a mesh: ctx: 64 (over y_lo, z, core), tp: 8 (over y_hi, x).
Axes of the slice: x: 4, y: 8 (y_hi: 2, y_lo: 4; y = y_hi * 4 + y_lo), z: 8, core: 2. Of those that a mesh axis runs over, the one named last changes fastest.
Arguments:
- tokens: bfloat16 [16384, 2048], P('ctx', 'tp'), may hold values from -6 to 6
- w_in: bfloat16 [2048, 4096], P('ctx', 'tp'), may hold values from -0.125 to 0.125
- w_bc: bfloat16 [2048, 2048], P('ctx', 'tp'), may hold values from -0.01171875 to 0.01171875
- w_dt: bfloat16 [2048, 64], P('ctx', 'tp'), may hold values from -0.125 to 0.125
- dt_bias: float32 [64], P('tp'), may hold values from -2 to 0
- decay_rate: float32 [64], P('tp'), may hold values from 1e-05 to 0.1
- skip_gain: float32 [64], P('tp'), may hold values from 0.5 to 1.5
- w_out: bfloat16 [4096, 2048], P('tp', 'ctx'), may hold values from -0.09375 to 0.09375
- cotangent: bfloat16 [16384, 2048], P('ctx', 'tp'), may hold values from -6 to 6
Outputs:
- output: bfloat16 [16384, 2048], P('ctx', 'tp')
- grad: bfloat16 [16384, 2048], P('ctx', 'tp')
All inputs are finite; a program needn't handle non-finite values.
Results may differ from a plain program's by a relative error of at most 0.0061.
Values may be sent and summed in bfloat16 or wider, within the bound.
No kernel may reach another device: no remote copies, remote signals or barrier semaphores. Data moves between devices by JAX's collectives and lax.ppermute only.
A program may use at most 128 MiB of HBM per device.

v0:
```python
import jax
import jax.numpy as jnp
from jax import lax
from jax.sharding import PartitionSpec as P

HEADDIM = 64
STATE = 128
SPAN = 256
HIGH = lax.Precision.HIGHEST


def carried_in(value, axis, combine, identity, reverse):
    devices, position = (lax.axis_size(axis), lax.axis_index(axis))
    everything = jax.tree.map(lambda part: lax.all_gather(part, axis), value)
    start = jax.tree.map(
        lambda part, zero: jnp.broadcast_to(jnp.asarray(zero, part.dtype), part.shape),
        value,
        identity,
    )

    def step(k, before):
        at = devices - 1 - k if reverse else k
        reached = at > position if reverse else at < position
        new = combine(before, jax.tree.map(lambda part: part[at], everything))
        return jax.tree.map(lambda a, b: jnp.where(reached, a, b), new, before)

    return lax.fori_loop(0, devices, step, start)


def ssd_core(values, b_rows, c_rows, step_size, decay_rate, state):
    length, heads, head_dim = values.shape
    groups = b_rows.shape[1]
    per_group = heads // groups
    blocks = length // SPAN
    lower_mask = (jnp.arange(SPAN)[:, None] >= jnp.arange(SPAN)[None, :])[None]

    def blocked(array):
        return array.reshape((blocks, SPAN) + array.shape[1:])

    def ssd_advance(carry, item):
        value_blk, b_blk, c_blk, step_blk = item
        cums = jnp.cumsum(-step_blk * decay_rate[None, :], axis=0)
        diff = cums.T[:, :, None] - cums.T[:, None, :]
        weight = jnp.where(lower_mask, jnp.exp(jnp.where(lower_mask, diff, 0.0)), 0.0)
        scores = jnp.einsum("tgn,sgn->gts", c_blk, b_blk, precision=HIGH)
        scores = jnp.repeat(scores, per_group, axis=0)
        inputs = step_blk[:, :, None] * value_blk
        inside = jnp.einsum("hts,shp->thp", scores * weight, inputs, precision=HIGH)
        c_head = jnp.repeat(c_blk, per_group, axis=1)
        b_head = jnp.repeat(b_blk, per_group, axis=1)
        carried = jnp.exp(cums)[:, :, None] * jnp.einsum(
            "thn,hpn->thp", c_head, carry, precision=HIGH
        )
        tail = jnp.exp(cums[-1][None, :] - cums)
        fresh = jnp.einsum("shp,shn->hpn", tail[:, :, None] * inputs, b_head, precision=HIGH)
        carry = jnp.exp(cums[-1])[:, None, None] * carry + fresh
        return (carry, inside + carried)

    final, outputs = lax.scan(
        jax.checkpoint(ssd_advance),
        state,
        (blocked(values), blocked(b_rows), blocked(c_rows), blocked(step_size)),
    )
    return (outputs.reshape(length, heads, head_dim), final)


def local_states(values, b_rows, step_size, decay_rate):
    length, heads, head_dim = values.shape
    groups = b_rows.shape[1]
    per_group = heads // groups
    blocks = length // SPAN

    def blocked(array):
        return array.reshape((blocks, SPAN) + array.shape[1:])

    def local_advance(carry, item):
        value_blk, b_blk, step_blk = item
        cums = jnp.cumsum(-step_blk * decay_rate[None, :], axis=0)
        tail = jnp.exp(cums[-1][None, :] - cums)
        b_head = jnp.repeat(b_blk, per_group, axis=1)
        inputs = (tail * step_blk)[:, :, None] * value_blk
        fresh = jnp.einsum("shp,shn->hpn", inputs, b_head, precision=HIGH)
        return (jnp.exp(cums[-1])[:, None, None] * carry + fresh, None)

    start = jnp.zeros((heads, head_dim, STATE), jnp.float32)
    final, unused = lax.scan(
        local_advance, start, (blocked(values), blocked(b_rows), blocked(step_size))
    )
    return final


def local_adjoint(d_mixed, c_rows, step_size, decay_rate):
    length, heads, head_dim = d_mixed.shape
    groups = c_rows.shape[1]
    per_group = heads // groups
    blocks = length // SPAN

    def blocked(array):
        return array.reshape((blocks, SPAN) + array.shape[1:])

    def retreat(carry, item):
        grad_blk, c_blk, step_blk = item
        cums = jnp.cumsum(-step_blk * decay_rate[None, :], axis=0)
        c_head = jnp.repeat(c_blk, per_group, axis=1)
        weighted = jnp.exp(cums)[:, :, None] * grad_blk
        term = jnp.einsum("thp,thn->hpn", weighted, c_head, precision=HIGH)
        return (term + jnp.exp(cums[-1])[:, None, None] * carry, None)

    start = jnp.zeros((heads, head_dim, STATE), jnp.float32)
    final, unused = lax.scan(
        retreat, start, (blocked(d_mixed), blocked(c_rows), blocked(step_size)), reverse=True
    )
    return final


def chain_combine(earlier, later):
    return (earlier[0] * later[0], later[0][:, None, None] * earlier[1] + later[1])


def per_device(tokens, w_in, w_bc, w_dt, dt_bias, decay_rate, skip_gain, w_out, cotangent):
    full_tokens = lax.all_gather(tokens, "tp", axis=1, tiled=True)
    rows = full_tokens.shape[0]
    heads = decay_rate.shape[0]
    inner = w_in.shape[1]
    pair_cols = w_bc.shape[1]
    groups = pair_cols // (2 * STATE)
    w_cat = jnp.concatenate([w_in, w_bc, w_dt], axis=1)
    whole_in, whole_out = (
        lax.all_gather(w_cat, "ctx", axis=0, tiled=True),
        lax.all_gather(w_out, "ctx", axis=1, tiled=True),
    )
    projected = jnp.dot(full_tokens, whole_in, preferred_element_type=jnp.float32)
    values = projected[:, :inner].astype(jnp.bfloat16)
    pairs = projected[:, inner : inner + pair_cols].astype(jnp.bfloat16)
    pre_step = projected[:, inner + pair_cols :] + dt_bias[None, :]
    step_size = jax.nn.softplus(pre_step)
    value_f = values.astype(jnp.float32).reshape(rows, heads, HEADDIM)
    paired = pairs.astype(jnp.float32).reshape(rows, groups, 2, STATE)
    b_rows = paired[:, :, 0]
    c_rows = paired[:, :, 1]
    zero_state = jnp.zeros((heads, HEADDIM, STATE), jnp.float32)
    end_state = local_states(value_f, b_rows, step_size, decay_rate)
    decay_total = jnp.exp(-jnp.sum(step_size * decay_rate[None, :], axis=0))
    unit_decay = jnp.ones_like(decay_total)
    state_in = carried_in(
        (decay_total, end_state), "ctx", chain_combine, (unit_decay, zero_state), False
    )[1]

    def with_state(vals, brows, crows, steps):
        return ssd_core(vals, brows, crows, steps, decay_rate, state_in)

    (core_out, core_end), pullback = jax.vjp(with_state, value_f, b_rows, c_rows, step_size)
    mixed = (
        (core_out + skip_gain[None, :, None] * value_f).reshape(rows, inner).astype(jnp.bfloat16)
    )
    partial_out = jnp.dot(mixed, whole_out, preferred_element_type=jnp.float32)
    output = lax.psum_scatter(partial_out, "tp", scatter_dimension=1, tiled=True).astype(
        jnp.bfloat16
    )
    full_cotangent = lax.all_gather(cotangent, "tp", axis=1, tiled=True)
    d_flat = lax.dot_general(
        full_cotangent, whole_out, (((1,), (1,)), ((), ())), preferred_element_type=jnp.float32
    )
    d_mixed = d_flat.reshape(rows, heads, HEADDIM)
    own_adjoint = local_adjoint(d_mixed, c_rows, step_size, decay_rate)
    adjoint = carried_in(
        (decay_total, own_adjoint), "ctx", chain_combine, (unit_decay, zero_state), True
    )[1]
    grads = pullback((d_mixed, adjoint))
    d_values = grads[0] + skip_gain[None, :, None] * d_mixed
    d_pre = grads[3] * jax.nn.sigmoid(pre_step)
    d_pairs = jnp.stack([grads[1], grads[2]], axis=2).reshape(rows, pair_cols)
    d_cat = jnp.concatenate(
        [
            d_values.reshape(rows, inner).astype(jnp.bfloat16),
            d_pairs.astype(jnp.bfloat16),
            d_pre.astype(jnp.bfloat16),
        ],
        axis=1,
    )
    partial_grad = lax.dot_general(
        d_cat, whole_in, (((1,), (1,)), ((), ())), preferred_element_type=jnp.float32
    )
    grad = lax.psum_scatter(partial_grad, "tp", scatter_dimension=1, tiled=True).astype(
        jnp.bfloat16
    )
    return (output, grad)


def solution(mesh):
    placed = (
        P("ctx", "tp"),
        P("ctx", "tp"),
        P("ctx", "tp"),
        P("ctx", "tp"),
        P("tp"),
        P("tp"),
        P("tp"),
        P("tp", "ctx"),
        P("ctx", "tp"),
    )
    return jax.shard_map(
        per_device,
        mesh=mesh,
        in_specs=placed,
        out_specs=(P("ctx", "tp"), P("ctx", "tp")),
        check_vma=False,
    )
```

profile of v0, /device:TPU:8, one launch (start us, length us, event | category | flops | bytes accessed | tf_op | source)
XLA Modules:
  0.0 956.6 jit_solution(10502070990085466387)
XLA Ops:
  8.7 1.4 pad_maximum_fusion.1
  11.5 70.3 %all-gather.12.cloned.1.call-done = bf16[256,2048]{1,0:T(8,128)(2,1)} async-done(((bf16[256,256]{1,0:T(8,128)(2,1)}), bf16[256,2048]{1,0:T(8,128)(2,1)}) %all-gather.12.cloned.1.call-update) | async-done | bytes 1048592 | tf_op jit(solution)/shard_map/all_gather | solution.py:121
  81.9 118.4 %all-gather.10.cloned.1.call-done = bf16[2048,776]{1,0:T(8,128)(2,1)} async-done(((bf16[32,776]{1,0:T(8,128)(2,1)}), bf16[2048,776]{1,0:T(8,128)(2,1)}) %all-gather.10.cloned.1.call-update) | async-done | bytes 3178512 | tf_op jit(solution)/shard_map/all_gather | solution.py:129
  200.3 3.5 fusion.87
  207.4 61.4 %all-gather.16.cloned.1.call-done = bf16[256,2048]{1,0:T(8,128)(2,1)} async-done(((bf16[256,256]{1,0:T(8,128)(2,1)}), bf16[256,2048]{1,0:T(8,128)(2,1)}) %all-gather.16.cloned.1.call-update) | async-done | bytes 1048592 | tf_op jit(solution)/shard_map/all_gather | solution.py:160
  268.9 115.9 %all-gather.14.cloned.1.call-done = bf16[512,2048]{0,1:T(8,128)(2,1)} async-done(((bf16[512,32]{0,1:T(8,128)(2,1)}), bf16[512,2048]{0,1:T(8,128)(2,1)}) %all-gather.14.cloned.1.call-update) | async-done | bytes 2097168 | tf_op jit(solution)/shard_map/all_gather | solution.py:130
  384.7 2.8 fusion.89
  387.7 1.4 convolution_add_fusion
  392.0 107.6 %all-reduce.2 = f32[512]{0:T(512)S(1)} all-reduce(f32[512]{0:T(512)S(1)} %exponential_dynamic-update-slice_fusion), channel_id=2, replica_groups=mesh['ctx'=64,'tp'=8] {'ctx'}, use_global_device_ids=true, to_apply=%add.2 | all-reduce | flops 512 | bytes 4096
  500.0 2.5 fusion.12
  502.5 16.9 %all-gather.18.cloned.1.call-done = f32[512,64,128]{2,1,0:T(8,128)} async-done(((f32[8,64,128]{2,1,0:T(8,128)}), f32[512,64,128]{2,1,0:T(8,128)}) %all-gather.18.cloned.1.call-update) | async-done | bytes 16777232 | tf_op jit(solution)/shard_map/all_gather | solution.py:14
  519.5 70.3 %while.22 = (s32[]{:T(128)}, f32[8,64,128]{2,1,0:T(8,128)S(1)}, s32[]{:T(128)}, f32[64,8]{1,0:T(8,128)S(1)}, f32[64,8,64,128]{3,2,1,0:T(8,128)}, /*index=5*/s32[]{:T(128)}, s32[]{:T(128)}) while((s32[]{:T(128)}, f32[8,64,128]{2,1,0:T(8,128)S(1)}, s32[]{:T(128)}, f32[64,8]{1,0:T(8,128)S(1)}, f32[64,8,64,128]{3,2,1,0:T(8,128)}, ...), condition=%wide.region_4.5_spmd.clone, body=%wide.region_3.4_spmd.clone.sunk | while | flops 262148 | bytes 786633 | solution.py:27
  589.7 66.3 %all-gather.20.cloned.1.call-done = f32[512,64,128]{2,1,0:T(8,128)} async-done(((f32[8,64,128]{2,1,0:T(8,128)}), f32[512,64,128]{2,1,0:T(8,128)}) %all-gather.20.cloned.1.call-update) | async-done | bytes 16777232 | tf_op jit(solution)/shard_map/all_gather | solution.py:14
  656.1 70.8 %while.23 = (s32[]{:T(128)}, f32[8,64,128]{2,1,0:T(8,128)S(1)}, s32[]{:T(128)}, f32[64,8]{1,0:T(8,128)S(1)}, f32[64,8,64,128]{3,2,1,0:T(8,128)}, /*index=5*/s32[]{:T(128)}, s32[]{:T(128)}, s32[]{:T(128)}, s32[]{:T(128)}) while((s32[]{:T(128)}, f32[8,64,128]{2,1,0:T(8,128)S(1)}, s32[]{:T(128)}, f32[64,8]{1,0:T(8,128)S(1)}, ...), condition=%wide.region_7.8_spmd.clone, body=%wide.region_6.7_spmd.clone.sunk | while | flops 262152 | bytes 786695 | solution.py:27
  730.0 3.1 fusion.22
  735.1 3.4 multiply_reduce_fusion.1
  740.2 2.7 reduce-window.44
  745.3 2.7 fusion.59
  748.0 1.5 copy-done.1
  749.5 2.1 fusion.88
  751.6 95.5 %reduce-scatter.5.cloned.1.call-done = f32[256,256]{1,0:T(8,128)} async-done(((f32[256,2048]{1,0:T(8,128)}), f32[256,256]{1,0:T(8,128)}) %reduce-scatter.5.cloned.1.call-update) | async-done | bytes 262160 | tf_op jit(solution)/shard_map/reduce_scatter | solution.py:184
  847.1 1.6 convert_element_type.31
  848.7 99.5 %reduce-scatter.3.cloned.1.call-done = f32[256,256]{1,0:T(8,128)} async-done(((f32[256,2048]{1,0:T(8,128)}), f32[256,256]{1,0:T(8,128)}) %reduce-scatter.3.cloned.1.call-update) | async-done | bytes 262160 | tf_op jit(solution)/shard_map/reduce_scatter | solution.py:157
  948.1 1.6 convert_element_type.27
  (351 shorter events, 154.7 us)
Async XLA Ops:
  7.2 74.7 %all-gather.12.cloned.1.call-start = ((), (), s32[]{:S(2)}) async-start(), calls=%async_computation.3 | async-start | bytes 1179648 | tf_op jit(solution)/shard_map/all_gather | solution.py:121
  7.9 192.4 %all-gather.10.cloned.1.call-start = ((), (), s32[]{:S(2)}) async-start(), calls=%async_computation.2 | async-start | bytes 3727360 | tf_op jit(solution)/shard_map/all_gather | solution.py:129
  10.1 258.7 %all-gather.16.cloned.1.call-start = ((), (), s32[]{:S(2)}) async-start(), calls=%async_computation.6 | async-start | bytes 1179648 | tf_op jit(solution)/shard_map/all_gather | solution.py:160
  10.9 373.9 %all-gather.14.cloned.1.call-start = ((), (), s32[]{:S(2)}) async-start(), calls=%async_computation.4 | async-start | bytes 2129920 | tf_op jit(solution)/shard_map/all_gather | solution.py:130
  11.5 192.3 %copy-start.3 = (f32[8]{0:T(128)S(1)}, f32[8]{0:T(128)}, u32[]{:S(2)}) copy-start(f32[8]{0:T(128)} %param.18) | copy-start | bytes 100
  11.5 192.3 %copy-start.6 = (f32[8]{0:T(128)S(1)}, f32[8]{0:T(128)}, u32[]{:S(2)}) copy-start(f32[8]{0:T(128)} %param.17) | copy-start | bytes 100
  11.5 508.0 %all-gather.18.cloned.1.call-start = ((), (), s32[]{:S(2)}) async-start(), calls=%async_computation.8 | async-start | bytes 17039360 | tf_op jit(solution)/shard_map/all_gather | solution.py:14
  203.7 0.9 copy-start.9
  207.4 181.8 %copy-start.8 = (f32[8]{0:T(128)S(1)}, f32[8]{0:T(128)}, u32[]{:S(2)}) copy-start(f32[8]{0:T(128)} %param.19) | copy-start | bytes 100
  207.4 448.7 %all-gather.20.cloned.1.call-start = ((), (), s32[]{:S(2)}) async-start(), calls=%async_computation.9 | async-start | bytes 17039360 | tf_op jit(solution)/shard_map/all_gather | solution.py:14
  389.1 458.0 %reduce-scatter.5.cloned.1.call-start = ((), (), s32[]{:S(2)}) async-start(), calls=%async_computation.7 | async-start | bytes 2359296 | tf_op jit(solution)/shard_map/reduce_scatter | solution.py:184
  738.5 5.7 copy-start.4
  738.5 5.7 copy-start.7
  738.5 6.5 copy-start.5
  738.9 6.2 copy-start.2
  743.0 2.2 copy-start
  747.9 1.6 copy-start.1
  748.0 200.2 %reduce-scatter.3.cloned.1.call-start = ((), (), s32[]{:S(2)}) async-start(), calls=%async_computation.5 | async-start | bytes 2359296 | tf_op jit(solution)/shard_map/reduce_scatter | solution.py:157
Sparse Core Ops, SparseCore 0:
  11.1 70.7 all-gather.11
  84.6 115.6 all-gather.9
  203.3 65.5 all-gather.15
  270.9 113.8 all-gather.13
  386.7 132.6 all-gather.17
  521.5 134.5 all-gather.19
  748.1 98.9 reduce-scatter.4
  852.4 95.7 reduce-scatter.2
where the time goes:
time: 961 us; the launch traced here: 957 us
  waiting for transfers between devices  646 us (67%)
  other arithmetic  146 us (15%)
  blocking collectives  108 us (11%)
  matrix products  28.9 us (3%)
  between operations  15.1 us (2%)
    select_n x128, other arithmetic, step(): return jax.tree.map(lambda a, b: jnp.where(reached, a, b), new, before)  135 us
    all_gather x1, waiting for transfers between devices, per_device(): lax.all_gather(w_cat, 'ctx', axis=0, tiled=True)  118 us
    all_gather x1, waiting for transfers between devices, per_device(): lax.all_gather(w_out, 'ctx', axis=1, tiled=True)  116 us
    unnamed x1, blocking collectives  108 us
    reduce_scatter x1, waiting for transfers between devices, per_device(): lax.psum_scatter(partial_out, 'tp', scatter_dimension=1, tiled=True)  99.5 us
    reduce_scatter x1, waiting for transfers between devices, per_device(): lax.psum_scatter(partial_grad, 'tp', scatter_dimension=1, tiled=True)  95.5 us
    all_gather x2, waiting for transfers between devices, carried_in(): everything = jax.tree.map(lambda part: lax.all_gather(part, axis), value)  83.3 us
    all_gather x1, waiting for transfers between devices, per_device(): full_tokens = lax.all_gather(tokens, 'tp', axis=1, tiled=True)  70.3 us
  transfers between devices with their start and end apart: 8, of which 8 were waited for; matrix products, arithmetic and copies ran while one was open for 9% of the time, Pallas kernels for 0%

commit v1 on v0

--- a/solution.py
+++ b/solution.py
@@ -118,7 +118,10 @@
 
 
 def per_device(tokens, w_in, w_bc, w_dt, dt_bias, decay_rate, skip_gain, w_out, cotangent):
-    full_tokens = lax.all_gather(tokens, "tp", axis=1, tiled=True)
+    size = lax.axis_size("tp")
+    shards = jnp.stack([tokens for _ in range(size)])
+    shards = lax.all_to_all(shards, "tp", split_axis=0, concat_axis=0)
+    full_tokens = jnp.concatenate(shards, axis=1)
     rows = full_tokens.shape[0]
     heads = decay_rate.shape[0]
     inner = w_in.shape[1]

time: 961 us -> 908 us (0.945)
  waiting for transfers between devices: 646 us -> 583 us
    all_gather x1 -> x0, waiting for transfers between devices: 70.3 us -> none  [per_device(): full_tokens = lax.all_gather(tokens, 'tp', axis=1, tiled=True)]
    all_to_all x0 -> x1, waiting for transfers between devices: none -> 30.6 us  [per_device(): shards = lax.all_to_all(shards, 'tp', split_axis=0, concat_axis=0)]
    all_gather x1, waiting for transfers between devices: 118 us -> 95.6 us  [per_device(): lax.all_gather(w_cat, 'ctx', axis=0, tiled=True)]
  transfers between devices with their start and end apart: 8 -> 8, of which waited for: 8 -> 8; matrix products, arithmetic and copies ran while one was open for 9% -> 10% of each run, Pallas kernels for 0% -> 0%
where the time goes in v1:
time: 908 us; the launch traced here: 904 us
  waiting for transfers between devices  583 us (64%)
  other arithmetic  146 us (16%)
  blocking collectives  108 us (12%)
  matrix products  28.6 us (3%)
  between operations  15.1 us (2%)
  local copies, waits for them, and re-layouts  9.57 us (1%)
    select_n x128, other arithmetic, step(): return jax.tree.map(lambda a, b: jnp.where(reached, a, b), new, before)  135 us
    all_gather x1, waiting for transfers between devices, per_device(): lax.all_gather(w_out, 'ctx', axis=1, tiled=True)  116 us
    unnamed x1, blocking collectives  108 us
    reduce_scatter x1, waiting for transfers between devices, per_device(): lax.psum_scatter(partial_out, 'tp', scatter_dimension=1, tiled=True)  99.5 us
    reduce_scatter x1, waiting for transfers between devices, per_device(): lax.psum_scatter(partial_grad, 'tp', scatter_dimension=1, tiled=True)  96.1 us
    all_gather x1, waiting for transfers between devices, per_device(): lax.all_gather(w_cat, 'ctx', axis=0, tiled=True)  95.6 us
    all_gather x2, waiting for transfers between devices, carried_in(): everything = jax.tree.map(lambda part: lax.all_gather(part, axis), value)  83.6 us
    all_gather x1, waiting for transfers between devices, per_device(): full_cotangent = lax.all_gather(cotangent, 'tp', axis=1, tiled=True)  60.1 us
  transfers between devices with their start and end apart: 8, of which 8 were waited for; matrix products, arithmetic and copies ran while one was open for 10% of the time, Pallas kernels for 0%

profile of v1, /device:TPU:8, one launch (start us, length us, event | category | flops | bytes accessed | tf_op | source)
XLA Modules:
  0.0 903.7 jit_solution(7668827267790254160)
XLA Ops:
  8.0 1.4 pad_maximum_fusion.1
  12.3 8.7 all-to-all-start
  21.7 30.6 %all-to-all-done = bf16[8,256,256]{1,2,0:T(8,128)(2,1)S(1)} async-done(((bf16[8,256,256]{1,2,0:T(8,128)(2,1)}), bf16[8,256,256]{1,2,0:T(8,128)(2,1)S(1)}, u32[]{:S(2)}, u32[]{:S(2)}) %all-to-all-start) | async-done | bytes 1048608 | tf_op jit(solution)/shard_map/all_to_all | solution.py:123
  52.3 95.6 %all-gather.9.cloned.1.call-done = bf16[2048,776]{1,0:T(8,128)(2,1)} async-done(((bf16[32,776]{1,0:T(8,128)(2,1)}), bf16[2048,776]{1,0:T(8,128)(2,1)}) %all-gather.9.cloned.1.call-update) | async-done | bytes 3178512 | tf_op jit(solution)/shard_map/all_gather | solution.py:132
  147.9 3.2 fusion.87
  154.8 60.1 %all-gather.13.cloned.1.call-done = bf16[256,2048]{1,0:T(8,128)(2,1)} async-done(((bf16[256,256]{1,0:T(8,128)(2,1)}), bf16[256,2048]{1,0:T(8,128)(2,1)}) %all-gather.13.cloned.1.call-update) | async-done | bytes 1048592 | tf_op jit(solution)/shard_map/all_gather | solution.py:163
  214.9 116.0 %all-gather.11.cloned.1.call-done = bf16[512,2048]{0,1:T(8,128)(2,1)} async-done(((bf16[512,32]{0,1:T(8,128)(2,1)}), bf16[512,2048]{0,1:T(8,128)(2,1)}) %all-gather.11.cloned.1.call-update) | async-done | bytes 2097168 | tf_op jit(solution)/shard_map/all_gather | solution.py:133
  330.9 2.8 fusion.89
  338.2 107.6 %all-reduce.2 = f32[512]{0:T(512)S(1)} all-reduce(f32[512]{0:T(512)S(1)} %exponential_dynamic-update-slice_fusion), channel_id=2, replica_groups=mesh['ctx'=64,'tp'=8] {'ctx'}, use_global_device_ids=true, to_apply=%add.2 | all-reduce | flops 512 | bytes 4096
  446.2 2.5 fusion.12
  448.7 17.4 %all-gather.15.cloned.1.call-done = f32[512,64,128]{2,1,0:T(8,128)} async-done(((f32[8,64,128]{2,1,0:T(8,128)}), f32[512,64,128]{2,1,0:T(8,128)}) %all-gather.15.cloned.1.call-update) | async-done | bytes 16777232 | tf_op jit(solution)/shard_map/all_gather | solution.py:14
  466.2 70.1 %while.22 = (s32[]{:T(128)}, f32[8,64,128]{2,1,0:T(8,128)S(1)}, s32[]{:T(128)}, f32[64,8]{1,0:T(8,128)S(1)}, f32[64,8,64,128]{3,2,1,0:T(8,128)}, /*index=5*/s32[]{:T(128)}, s32[]{:T(128)}) while((s32[]{:T(128)}, f32[8,64,128]{2,1,0:T(8,128)S(1)}, s32[]{:T(128)}, f32[64,8]{1,0:T(8,128)S(1)}, f32[64,8,64,128]{3,2,1,0:T(8,128)}, ...), condition=%wide.region_4.5_spmd.clone, body=%wide.region_3.4_spmd.clone.sunk | while | flops 262148 | bytes 786633 | solution.py:27
  536.3 66.2 %all-gather.17.cloned.1.call-done = f32[512,64,128]{2,1,0:T(8,128)} async-done(((f32[8,64,128]{2,1,0:T(8,128)}), f32[512,64,128]{2,1,0:T(8,128)}) %all-gather.17.cloned.1.call-update) | async-done | bytes 16777232 | tf_op jit(solution)/shard_map/all_gather | solution.py:14
  602.5 70.8 %while.23 = (s32[]{:T(128)}, f32[8,64,128]{2,1,0:T(8,128)S(1)}, s32[]{:T(128)}, f32[64,8]{1,0:T(8,128)S(1)}, f32[64,8,64,128]{3,2,1,0:T(8,128)}, /*index=5*/s32[]{:T(128)}, s32[]{:T(128)}, s32[]{:T(128)}, s32[]{:T(128)}) while((s32[]{:T(128)}, f32[8,64,128]{2,1,0:T(8,128)S(1)}, s32[]{:T(128)}, f32[64,8]{1,0:T(8,128)S(1)}, ...), condition=%wide.region_7.8_spmd.clone, body=%wide.region_6.7_spmd.clone.sunk | while | flops 262152 | bytes 786695 | solution.py:27
  676.5 3.1 fusion.22
  681.6 3.4 multiply_reduce_fusion.1
  686.6 2.7 reduce-window.44
  691.7 2.7 fusion.59
  694.4 1.5 copy-done.1
  695.9 2.1 fusion.88
  698.0 96.1 %reduce-scatter.5.cloned.1.call-done = f32[256,256]{1,0:T(8,128)} async-done(((f32[256,2048]{1,0:T(8,128)}), f32[256,256]{1,0:T(8,128)}) %reduce-scatter.5.cloned.1.call-update) | async-done | bytes 262160 | tf_op jit(solution)/shard_map/reduce_scatter | solution.py:187
  794.1 1.6 convert_element_type.31
  795.8 99.5 %reduce-scatter.3.cloned.1.call-done = f32[256,256]{1,0:T(8,128)} async-done(((f32[256,2048]{1,0:T(8,128)}), f32[256,256]{1,0:T(8,128)}) %reduce-scatter.3.cloned.1.call-update) | async-done | bytes 262160 | tf_op jit(solution)/shard_map/reduce_scatter | solution.py:160
  895.2 1.6 convert_element_type.27
  (352 shorter events, 157.5 us)
Async XLA Ops:
  7.2 140.7 %all-gather.9.cloned.1.call-start = ((), (), s32[]{:S(2)}) async-start(), calls=%async_computation.3 | async-start | bytes 3727360 | tf_op jit(solution)/shard_map/all_gather | solution.py:132
  9.4 205.5 %all-gather.13.cloned.1.call-start = ((), (), s32[]{:S(2)}) async-start(), calls=%async_computation.6 | async-start | bytes 1179648 | tf_op jit(solution)/shard_map/all_gather | solution.py:163
  12.3 40.0 %all-to-all-start = ((bf16[8,256,256]{1,2,0:T(8,128)(2,1)}), bf16[8,256,256]{1,2,0:T(8,128)(2,1)S(1)}, u32[]{:S(2)}, u32[]{:S(2)}) async-start(bf16[8,256,256]{1,2,0:T(8,128)(2,1)} %stack.5), calls=%async_computation | async-start | bytes 2097152 | tf_op jit(solution)/shard_map/all_to_all | solution.py:123
  20.9 310.0 %all-gather.11.cloned.1.call-start = ((), (), s32[]{:S(2)}) async-start(), calls=%async_computation.4 | async-start | bytes 2129920 | tf_op jit(solution)/shard_map/all_gather | solution.py:133
  21.7 444.5 %all-gather.15.cloned.1.call-start = ((), (), s32[]{:S(2)}) async-start(), calls=%async_computation.8 | async-start | bytes 17039360 | tf_op jit(solution)/shard_map/all_gather | solution.py:14
  147.9 3.2 copy-start.3
  147.9 3.2 copy-start.6
  151.1 0.9 copy-start.9
  154.8 180.6 %copy-start.8 = (f32[8]{0:T(128)S(1)}, f32[8]{0:T(128)}, u32[]{:S(2)}) copy-start(f32[8]{0:T(128)} %param.19) | copy-start | bytes 100
  154.8 447.7 %all-gather.17.cloned.1.call-start = ((), (), s32[]{:S(2)}) async-start(), calls=%async_computation.9 | async-start | bytes 17039360 | tf_op jit(solution)/shard_map/all_gather | solution.py:14
  335.3 458.8 %reduce-scatter.5.cloned.1.call-start = ((), (), s32[]{:S(2)}) async-start(), calls=%async_computation.7 | async-start | bytes 2359296 | tf_op jit(solution)/shard_map/reduce_scatter | solution.py:187
  684.9 5.7 copy-start.4
  684.9 5.7 copy-start.7
  684.9 6.5 copy-start.5
  685.3 6.2 copy-start.2
  689.4 2.2 copy-start
  694.3 1.6 copy-start.1
  694.4 200.9 %reduce-scatter.3.cloned.1.call-start = ((), (), s32[]{:S(2)}) async-start(), calls=%async_computation.5 | async-start | bytes 2359296 | tf_op jit(solution)/shard_map/reduce_scatter | solution.py:160
Sparse Core Ops, SparseCore 0:
  10.7 137.1 all-gather.8
  150.9 63.9 all-gather.12
  217.1 113.8 all-gather.10
  332.9 133.1 all-gather.14
  468.1 134.2 all-gather.16
  694.5 99.6 reduce-scatter.4
  799.5 95.7 reduce-scatter.2
